TPU v7x, 32 devices: a whole 2x2x4 slice. The times are simulated.
32 devices in a mesh: groups: 2 (over y), enc: 4 (over z), mp: 4 (over x, core).
Axes of the slice: x: 2, y: 2, z: 4, core: 2. Of those that a mesh axis runs over, the one named last changes fastest.
Arguments:
- hidden: bfloat16 [131072, 1024], P(('groups', 'enc'), 'mp'), parts along dimension 0, may hold values from -6 to 6
- proj_w: bfloat16 [1024, 128], P('mp'), may hold values from -0.1875 to 0.1875
- queries: bfloat16 [256, 32, 128], P(('groups', 'enc', 'mp')), parts along dimension 0, may hold values from -208 to 208
- lengths: int32 [512], P('groups'), parts along dimension 0, may hold values from 193 to 256, as said below
- candidates: int32 [256, 16], P(('groups', 'enc', 'mp')), parts along dimension 0, may hold values from 0 to 1023, as said below
Outputs:
- losses: float32 [256], P(('groups', 'enc', 'mp')), parts along dimension 0
- grad_w: float32 [2048, 128], P(('groups', 'mp')), parts along dimension 0
There are 2 independent parts, one for each index of `groups`. A program takes and returns all parts, laid end to end along the dimension named above; an argument that names none is the same for every part. Nothing has to cross between parts.
Inputs may be any that keep to these rules, and one draw needn't show every extreme that they name: Entries are global block numbers of this part. Of the candidates of the 8 queries of one device (aligned rows), at most 16 lie in the 64 blocks of any one device along enc+mp, where device k holds blocks k * 64 to (k + 1) * 64 - 1; some device receives exactly 16 from every device. Blocks may repeat. `lengths`: some passage has 256 tokens and some has 193.
All inputs are finite; a program needn't handle non-finite values.
Results may differ from a plain program's by a relative error of at most 0.0013.
The roundings to bfloat16 on the way count: a program that leaves them out, or rounds other values in their place, can miss the bound.
Values may be sent and summed in bfloat16 or wider, within the bound.
No kernel may reach another device: no remote copies, remote signals or barrier semaphores. Data moves between devices by JAX's collectives and lax.ppermute only.
A program may use at most 128 MiB of HBM per device.

v0:
```python
import jax
import jax.numpy as jnp
from jax import lax
from jax.sharding import PartitionSpec as P

L = 256
BLK = 64


def block_valid(block_ids, lengths):
    per_passage = L // BLK
    passage = block_ids // per_passage
    within = block_ids % per_passage
    positions = within[..., None] * BLK + jnp.arange(BLK, dtype=jnp.int32)
    return positions < lengths[passage][..., None]


def soft_max_sim(sim_tile, valid_mask):
    masked = jnp.where(valid_mask, sim_tile, jnp.float32(-1e30))
    peak = jnp.max(masked, -1, keepdims=True)
    shifted = jnp.exp(masked - peak)
    running = jnp.sum(shifted, -1, keepdims=True)
    scores = jnp.mean(peak[..., 0] + jnp.log(running[..., 0]), -1)
    weights = (shifted / running).astype(jnp.bfloat16)
    return (scores, weights)


def loss_terms(scores):
    margins = scores[:, 1:] - scores[:, :1]
    losses = jnp.mean(jax.nn.softplus(margins), 1)
    slopes = jax.nn.sigmoid(margins) / (scores.shape[1] - 1)
    d_score = jnp.concatenate([-jnp.sum(slopes, 1, keepdims=True), slopes], 1)
    return (losses, d_score)


def left_product(left, right):
    return lax.dot_general(
        left, right, (((0,), (0,)), ((), ())), preferred_element_type=jnp.float32
    )


def local(hidden, proj_w, queries, lengths, candidates):
    mp_count = lax.axis_size("mp")
    owners = lax.axis_size("enc") * mp_count
    row_share = hidden.shape[0] // mp_count
    emb_width = proj_w.shape[1]
    qry_dev = queries.shape[0]
    query_len = queries.shape[1]
    cand_count = candidates.shape[1]
    blk_dev = row_share // BLK
    slot_count = qry_dev * cand_count
    capacity = 2 * slot_count // owners
    e_pre = lax.psum_scatter(
        jnp.dot(hidden, proj_w, preferred_element_type=jnp.float32),
        "mp",
        scatter_dimension=0,
        tiled=True,
    )
    scale = lax.rsqrt(jnp.sum(e_pre * e_pre, -1, keepdims=True) + 1e-06)
    embedded = (e_pre * scale).astype(jnp.bfloat16)
    local_blocks = embedded.reshape(blk_dev, BLK, emb_width)
    flat_cand = candidates.reshape(-1)
    owner_of = flat_cand // blk_dev
    slot_ids = jnp.arange(slot_count, dtype=jnp.int32)
    same_owner = owner_of[:, None] == owner_of[None, :]
    earlier = slot_ids[None, :] < slot_ids[:, None]
    rank_in = jnp.sum(jnp.where(same_owner & earlier, 1, 0), 1).astype(jnp.int32)
    dest = owner_of * capacity + rank_in
    wanted = jnp.zeros((owners * capacity,), jnp.int32).at[dest].set(flat_cand % blk_dev)
    served = lax.all_to_all(
        wanted.reshape(owners, capacity), ("enc", "mp"), split_axis=0, concat_axis=0, tiled=True
    ).reshape(-1)
    grad_emb = jnp.zeros((blk_dev, BLK, emb_width), jnp.float32)
    tiles = local_blocks[served].reshape(owners, capacity, BLK, emb_width)
    arrived = lax.all_to_all(tiles, ("enc", "mp"), split_axis=0, concat_axis=0, tiled=True).reshape(
        owners * capacity, BLK, emb_width
    )
    mine = arrived[dest].reshape(qry_dev, cand_count, BLK, emb_width)
    valid_mask = block_valid(candidates, lengths)
    sim_tile = jnp.einsum("qie,qcje->qcij", queries, mine, preferred_element_type=jnp.float32)
    scores, weights = soft_max_sim(sim_tile, valid_mask[:, :, None, :])
    losses, d_score = loss_terms(scores)
    occ_grad = jnp.einsum("qcij,qie->qcje", weights, queries, preferred_element_type=jnp.float32)
    occ_grad = (occ_grad * (d_score / query_len)[:, :, None, None]).astype(jnp.bfloat16)
    outgoing = jnp.zeros((owners * capacity, BLK, emb_width), jnp.bfloat16)
    outgoing = outgoing.at[dest].set(occ_grad.reshape(slot_count, BLK, emb_width))
    returned = lax.all_to_all(
        outgoing.reshape(owners, capacity, BLK, emb_width),
        ("enc", "mp"),
        split_axis=0,
        concat_axis=0,
        tiled=True,
    )
    grad_emb = grad_emb.at[served].add(returned.reshape(-1, BLK, emb_width).astype(jnp.float32))
    grad_flat = grad_emb.reshape(row_share, emb_width)
    dot_e = jnp.sum(e_pre * grad_flat, -1, keepdims=True)
    de_pre = (scale * grad_flat - e_pre * (scale * scale * scale) * dot_e).astype(jnp.bfloat16)
    partial_w = left_product(hidden, lax.all_gather(de_pre, "mp", axis=0, tiled=True))
    grad_w = lax.psum(partial_w, "enc")
    return (losses, grad_w)


def solution(mesh):
    return jax.shard_map(
        local,
        mesh=mesh,
        in_specs=(
            P(("groups", "enc"), "mp"),
            P("mp", None),
            P(("groups", "enc", "mp"), None, None),
            P("groups"),
            P(("groups", "enc", "mp"), None),
        ),
        out_specs=(P(("groups", "enc", "mp")), P(("groups", "mp"), None)),
        check_vma=False,
    )
```

profile of v0, /device:TPU:0, one launch (start us, length us, event | category | flops | bytes accessed | tf_op | source)
XLA Modules:
  0.0 446.6 jit_solution(9475051947328319691)
XLA Ops:
  7.2 0.0 copy-start
  7.2 0.0 reduce-scatter.2.cloned.1.call-start
  7.2 0.8 copy-done
  8.0 8.9 %fusion.22 = f32[16384,128]{1,0:T(8,128)} fusion(bf16[16384,256]{1,0:T(8,128)(2,1)} %param.5, bf16[256,128]{1,0:T(8,128)(2,1)S(1)} %copy-done), kind=kOutput, calls=%fused_computation.74 | convolution fusion | flops 1073741824 | bytes 16842752 | tf_op jit(solution)/shard_map/dot_general | solution.py:54
  16.9 0.0 copy-start.6
  16.9 0.0 reduce-scatter.2.cloned.1.call-update
  17.0 0.7 copy-done.6
  17.6 0.1 reshape.243
  17.7 0.1 reshape.242
  17.8 0.2 select_reduce_fusion
  18.0 1.0 scatter_custom_fusion
  19.0 0.1 all_to_all.12
  19.1 13.6 %all_to_all.19 = s32[16,1,16]{2,1,0:T(1,128)S(1)} all-to-all(s32[16,1,16]{2,1,0:T(1,128)S(1)} %all_to_all.12), channel_id=1, replica_groups=mesh['groups'=2,'enc'=4,'mp'=4] {'enc','mp'}, dimensions={0} | all-to-all | bytes 2048 | tf_op jit(solution)/shard_map/all_to_all | solution.py:70
  32.7 0.5 broadcast.263
  33.2 0.7 reduce.5
  33.8 0.1 reshape.244
  33.9 57.6 %reduce-scatter.2.cloned.1.call-done = f32[4096,128]{1,0:T(8,128)} async-done(((f32[16384,128]{1,0:T(8,128)}), f32[4096,128]{1,0:T(8,128)}) %reduce-scatter.2.cloned.1.call-update) | async-done | bytes 2097168 | tf_op jit(solution)/shard_map/reduce_scatter | solution.py:53
  91.5 0.0 copy-start.2
  91.5 2.4 multiply_reduce_fusion
  93.9 0.0 copy-done.2
  93.9 0.7 multiply_convert_fusion.1
  94.6 3.1 gather_fusion.1
  97.7 4.8 %all-to-all-start.1 = ((bf16[16,16,64,128]{3,2,1,0:T(8,128)(2,1)}), bf16[16,16,64,128]{3,2,1,0:T(8,128)(2,1)}, u32[]{:S(2)}, u32[]{:S(2)}) async-start(bf16[16,16,64,128]{3,2,1,0:T(8,128)(2,1)} %bitcast.55), calls=%async_computation.2 | async-start | bytes 8388608 | tf_op jit(solution)/shard_map/all_to_all | solution.py:75
  102.5 0.0 copy-start.1
  102.5 0.0 all-gather.2.cloned.1.call-start
  102.6 0.1 reshape.254
  102.7 0.5 copy-done.1
  103.2 1.3 gather_fusion
  104.5 0.1 reshape.253
  104.5 0.1 add_compare_fusion
  104.7 75.5 %all-to-all-done.1 = bf16[16,16,64,128]{3,2,1,0:T(8,128)(2,1)} async-done(((bf16[16,16,64,128]{3,2,1,0:T(8,128)(2,1)}), bf16[16,16,64,128]{3,2,1,0:T(8,128)(2,1)}, u32[]{:S(2)}, u32[]{:S(2)}) %all-to-all-start.1) | async-done | bytes 4194336 | tf_op jit(solution)/shard_map/all_to_all | solution.py:75
  180.2 0.0 copy-start.5
  180.2 4.4 gather_fusion.2
  184.5 0.0 copy-done.5
  184.5 3.8 bitcast_reduce_fusion
  188.3 1.3 fusion.4
  189.6 0.1 add_reduce_fusion
  189.7 0.1 slice_reduce_fusion
  189.8 0.2 fusion.21
  190.1 0.1 copy.15
  190.2 0.1 maximum_multiply_fusion
  190.3 4.4 multiply_convert_fusion
  194.7 0.0 copy-start.4
  194.7 3.0 broadcast_in_dim.32
  197.7 0.0 copy-done.4
  197.7 15.7 %scatter_fusion = bf16[256,64,128]{2,1,0:T(8,128)(2,1)} fusion(bf16[256,64,128]{2,1,0:T(8,128)(2,1)} %broadcast_in_dim.32, s32[128]{0:T(128)S(1)} %fusion.17, bf16[128,64,128]{2,1,0:T(8,128)(2,1)S(1)} %bitcast.57), kind=kCustom, calls=%fused_computation.4 | custom fusion | bytes 6291968 | tf_op jit(solution)/shard_map/scatter | solution.py:86
  213.4 111.9 %all_to_all.20 = bf16[16,16,64,128]{3,2,1,0:T(8,128)(2,1)S(1)} all-to-all(bf16[16,16,64,128]{3,2,1,0:T(8,128)(2,1)} %bitcast.53), channel_id=1, replica_groups=mesh['groups'=2,'enc'=4,'mp'=4] {'enc','mp'}, dimensions={0} | all-to-all | bytes 8388608 | tf_op jit(solution)/shard_map/all_to_all | solution.py:87
  325.3 4.5 %bitcast_convert_fusion = f32[256,64,128]{2,1,0:T(8,128)} fusion(bf16[16,16,64,128]{3,2,1,0:T(8,128)(2,1)S(1)} %all_to_all.20), kind=kLoop, calls=%fused_computation.6 | loop fusion | flops 2097152 | bytes 12582912 | tf_op jit(solution)/shard_map/convert_element_type | solution.py:94
  329.8 0.2 broadcast_in_dim.31
  330.1 26.3 %scatter_fusion.1 = f32[64,64,128]{2,1,0:T(8,128)S(1)} fusion(f32[64,64,128]{2,1,0:T(8,128)S(1)} %broadcast_in_dim.31, s32[256]{0:T(256)S(1)} %bitcast.59, f32[256,64,128]{2,1,0:T(8,128)} %bitcast_convert_fusion), kind=kCustom, calls=%fused_computation.5 | custom fusion | flops 2097152 | bytes 25166848 | tf_op jit(solution)/shard_map/scatter-add | solution.py:94
  356.3 0.0 copy-start.3
  356.3 2.4 fusion.2
  358.7 0.0 copy-done.3
  358.7 3.0 fusion.1
  361.7 0.0 all-gather.2.cloned.1.call-update
  361.7 0.0 all-reduce.2.cloned.1.call-start
  361.8 35.2 %all-gather.2.cloned.1.call-done = bf16[16384,128]{1,0:T(8,128)(2,1)} async-done(((bf16[4096,128]{1,0:T(8,128)(2,1)}), bf16[16384,128]{1,0:T(8,128)(2,1)}) %all-gather.2.cloned.1.call-update) | async-done | bytes 4194320 | tf_op jit(solution)/shard_map/all_gather | solution.py:98
  397.0 6.8 %convolution_bitcast_fusion = f32[256,128]{0,1:T(8,128)} fusion(bf16[16384,128]{1,0:T(8,128)(2,1)} %all-gather.2.cloned.1.call-done, bf16[16384,256]{1,0:T(8,128)(2,1)} %param.5), kind=kOutput, calls=%fused_computation.20 | convolution fusion | flops 1073741824 | bytes 12713984 | tf_op jit(solution)/shard_map/dot_general | solution.py:37
  403.8 0.0 all-reduce.2.cloned.1.call-update
  403.8 0.5 broadcast_multiply_fusion.1
  404.3 34.1 %all-reduce.2.cloned.1.call-done = f32[256,128]{0,1:T(8,128)} async-done(((f32[256,128]{0,1:T(8,128)}), f32[256,128]{0,1:T(8,128)}) %all-reduce.2.cloned.1.call-update) | async-done | bytes 131088 | tf_op jit(solution)/shard_map/psum | solution.py:99
  438.4 1.7 copy.16
  (10 shorter events, 0.1 us)
Async XLA Ops:
  7.2 0.8 copy-start
  7.2 84.4 %reduce-scatter.2.cloned.1.call-start = ((), (), s32[]{:S(2)}) async-start(), calls=%async_computation.4 | async-start | bytes 10485760 | tf_op jit(solution)/shard_map/reduce_scatter | solution.py:53
  16.9 0.7 copy-start.6
  91.5 2.4 copy-start.2
  97.7 82.5 %all-to-all-start.1 = ((bf16[16,16,64,128]{3,2,1,0:T(8,128)(2,1)}), bf16[16,16,64,128]{3,2,1,0:T(8,128)(2,1)}, u32[]{:S(2)}, u32[]{:S(2)}) async-start(bf16[16,16,64,128]{3,2,1,0:T(8,128)(2,1)} %bitcast.55), calls=%async_computation.2 | async-start | bytes 8388608 | tf_op jit(solution)/shard_map/all_to_all | solution.py:75
  102.5 0.7 copy-start.1
  102.5 294.4 %all-gather.2.cloned.1.call-start = ((), (), s32[]{:S(2)}) async-start(), calls=%async_computation.5 | async-start | bytes 5242880 | tf_op jit(solution)/shard_map/all_gather | solution.py:98
  180.2 4.4 copy-start.5
  194.7 3.0 copy-start.4
  356.3 2.4 copy-start.3
  361.7 76.7 %all-reduce.2.cloned.1.call-start = ((), (), s32[]{:S(2)}) async-start(), calls=%async_computation.6 | async-start | bytes 262144 | tf_op jit(solution)/shard_map/psum | solution.py:99
Sparse Core Ops, SparseCore 0:
  17.1 74.3 reduce-scatter.1
  361.8 35.0 all-gather.1
  403.9 34.4 all-reduce.1
where the time goes:
time: 448 us; the launch traced here: 447 us
  waiting for transfers between devices  202 us (45%)
  blocking collectives  125 us (28%)
  other arithmetic  42.4 us (9%)
  local copies, waits for them, and re-layouts  33.4 us (7%)
  matrix products  24 us (5%)
  between operations  14 us (3%)
  starting transfers between devices  4.9 us (1%)
    all_to_all x1, blocking collectives, local(): lax.all_to_all(outgoing.reshape(owners, capacity, BLK, emb_width), ('enc'...  112 us
    all_to_all x1, waiting for transfers between devices, local(): lax.all_to_all(tiles, ('enc', 'mp'), split_axis=0, concat_axis=0, tiled=T...  75.5 us
    reduce_scatter x1, waiting for transfers between devices, local(): lax.psum_scatter(jnp.dot(hidden, proj_w, preferred_element_type=jnp.float...  57.6 us
    all_gather x1, waiting for transfers between devices, local(): lax.all_gather(de_pre, 'mp', axis=0, tiled=True)  35.2 us
    psum x1, waiting for transfers between devices, local(): grad_w = lax.psum(partial_w, 'enc')  34.1 us
    scatter-add x1, other arithmetic, local(): grad_emb.at[served]  26.3 us
    scatter x1, local copies, waits for them, and re-layouts, local(): outgoing.at[dest].set(occ_grad.reshape(slot_count, BLK, emb_width))  15.7 us
    all_to_all x1, blocking collectives, local(): lax.all_to_all(wanted.reshape(owners, capacity), ('enc', 'mp'), split_axi...  13.6 us
  transfers between devices with their start and end apart: 4, of which 4 were waited for; matrix products, arithmetic and copies ran while one was open for 1% of the time, Pallas kernels for 0%

commit v1 on v0

--- a/solution.py
+++ b/solution.py
@@ -5,6 +5,19 @@
 
 L = 256
 BLK = 64
+
+
+def collect(x, axis, dim):
+    size, index, width = (lax.axis_size(axis), lax.axis_index(axis), x.shape[dim])
+    upward = [(i, (i + 1) % size) for i in range(size)]
+    out = jnp.zeros((*x.shape[:dim], size * width, *x.shape[dim + 1 :]), x.dtype)
+    held = x
+    for step in range(size):
+        owner = (index - step) % size
+        out = lax.dynamic_update_slice_in_dim(out, held, owner * width, axis=dim)
+        if step < size - 1:
+            held = lax.ppermute(held, axis, upward)
+    return out
 
 
 def block_valid(block_ids, lengths):
@@ -95,7 +108,7 @@
     grad_flat = grad_emb.reshape(row_share, emb_width)
     dot_e = jnp.sum(e_pre * grad_flat, -1, keepdims=True)
     de_pre = (scale * grad_flat - e_pre * (scale * scale * scale) * dot_e).astype(jnp.bfloat16)
-    partial_w = left_product(hidden, lax.all_gather(de_pre, "mp", axis=0, tiled=True))
+    partial_w = left_product(hidden, collect(de_pre, "mp", 0))
     grad_w = lax.psum(partial_w, "enc")
     return (losses, grad_w)
 

time: 448 us -> 463 us (1.033)
  blocking collectives: 125 us -> 13.6 us
  waiting for transfers between devices: 202 us -> 299 us
  starting transfers between devices: 4.9 us -> 25.5 us
  local copies, waits for them, and re-layouts: 33.4 us -> 40.2 us
    all_to_all x1 -> x0, blocking collectives: 112 us -> none  [local(): lax.all_to_all(outgoing.reshape(owners, capacity, BLK, emb_width), ('enc'...]
    all_to_all x0 -> x1, waiting for transfers between devices: none -> 77.4 us  [local(): lax.all_to_all(outgoing.reshape(owners, capacity, BLK, emb_width), ('enc'...]
    ppermute x0 -> x3, waiting for transfers between devices: none -> 44.6 us  [collect(): held = lax.ppermute(held, axis, upward)]
    all_gather x1 -> x0, waiting for transfers between devices: 35.2 us -> none  [local(): lax.all_gather(de_pre, 'mp', axis=0, tiled=True)]
    all_to_all x0 -> x1, starting transfers between devices: none -> 19.7 us  [local(): lax.all_to_all(outgoing.reshape(owners, capacity, BLK, emb_width), ('enc'...]
    psum x1, waiting for transfers between devices: 34.1 us -> 44.1 us  [local(): grad_w = lax.psum(partial_w, 'enc')]
  transfers between devices with their start and end apart: 4 -> 7, of which waited for: 4 -> 7; matrix products, arithmetic and copies ran while one was open for 1% -> 1% of each run, Pallas kernels for 0% -> 0%
where the time goes in v1:
time: 463 us; the launch traced here: 461 us
  waiting for transfers between devices  299 us (65%)
  other arithmetic  43.9 us (9%)
  local copies, waits for them, and re-layouts  40.2 us (9%)
  starting transfers between devices  25.5 us (6%)
  matrix products  24 us (5%)
  between operations  14.3 us (3%)
  blocking collectives  13.6 us (3%)
    all_to_all x1, waiting for transfers between devices, local(): lax.all_to_all(outgoing.reshape(owners, capacity, BLK, emb_width), ('enc'...  77.4 us
    all_to_all x1, waiting for transfers between devices, local(): lax.all_to_all(tiles, ('enc', 'mp'), split_axis=0, concat_axis=0, tiled=T...  75.5 us
    reduce_scatter x1, waiting for transfers between devices, local(): lax.psum_scatter(jnp.dot(hidden, proj_w, preferred_element_type=jnp.float...  57.6 us
    ppermute x3, waiting for transfers between devices, collect(): held = lax.ppermute(held, axis, upward)  44.6 us
    psum x1, waiting for transfers between devices, local(): grad_w = lax.psum(partial_w, 'enc')  44.1 us
    scatter-add x1, other arithmetic, local(): grad_emb.at[served]  26.3 us
    all_to_all x1, starting transfers between devices, local(): lax.all_to_all(outgoing.reshape(owners, capacity, BLK, emb_width), ('enc'...  19.7 us
    scatter x1, local copies, waits for them, and re-layouts, local(): outgoing.at[dest].set(occ_grad.reshape(slot_count, BLK, emb_width))  15.7 us
  transfers between devices with their start and end apart: 7, of which 7 were waited for; matrix products, arithmetic and copies ran while one was open for 1% of the time, Pallas kernels for 0%

profile of v1, /device:TPU:0, one launch (start us, length us, event | category | flops | bytes accessed | tf_op | source)
XLA Modules:
  0.0 460.7 jit_solution(7581959835115146656)
XLA Ops:
  7.2 0.0 copy-start
  7.2 0.0 reduce-scatter.2.cloned.1.call-start
  7.2 0.8 copy-done
  8.0 8.9 %fusion.22 = f32[16384,128]{1,0:T(8,128)} fusion(bf16[16384,256]{1,0:T(8,128)(2,1)} %param.5, bf16[256,128]{1,0:T(8,128)(2,1)S(1)} %copy-done), kind=kOutput, calls=%fused_computation.78 | convolution fusion | flops 1073741824 | bytes 16842752 | tf_op jit(solution)/shard_map/dot_general | solution.py:67
  16.9 0.0 reduce-scatter.2.cloned.1.call-update
  17.0 0.7 copy-done.7
  17.6 0.1 reshape.243
  17.7 0.1 reshape.242
  17.8 0.2 select_reduce_fusion
  18.0 1.0 scatter_custom_fusion
  19.0 0.1 all_to_all.12
  19.1 13.6 %all_to_all.19 = s32[16,1,16]{2,1,0:T(1,128)S(1)} all-to-all(s32[16,1,16]{2,1,0:T(1,128)S(1)} %all_to_all.12), channel_id=1, replica_groups=mesh['groups'=2,'enc'=4,'mp'=4] {'enc','mp'}, dimensions={0} | all-to-all | bytes 2048 | tf_op jit(solution)/shard_map/all_to_all | solution.py:83
  32.7 0.5 broadcast.267
  33.2 0.7 reduce.5
  33.8 0.1 reshape.244
  33.9 57.6 %reduce-scatter.2.cloned.1.call-done = f32[4096,128]{1,0:T(8,128)} async-done(((f32[16384,128]{1,0:T(8,128)}), f32[4096,128]{1,0:T(8,128)}) %reduce-scatter.2.cloned.1.call-update) | async-done | bytes 2097168 | tf_op jit(solution)/shard_map/reduce_scatter | solution.py:66
  91.5 2.4 multiply_reduce_fusion
  93.9 0.0 copy-done.2
  93.9 0.7 multiply_convert_fusion.1
  94.6 3.1 gather_fusion.1
  97.7 4.8 %all-to-all-start.1 = ((bf16[16,16,64,128]{3,2,1,0:T(8,128)(2,1)}), bf16[16,16,64,128]{3,2,1,0:T(8,128)(2,1)}, u32[]{:S(2)}, u32[]{:S(2)}) async-start(bf16[16,16,64,128]{3,2,1,0:T(8,128)(2,1)} %bitcast.55), calls=%async_computation.2 | async-start | bytes 8388608 | tf_op jit(solution)/shard_map/all_to_all | solution.py:88
  102.5 0.0 copy-start.1
  102.5 0.1 reshape.254
  102.6 0.6 copy-done.1
  103.2 1.3 gather_fusion
  104.5 0.1 reshape.253
  104.5 0.1 add_compare_fusion
  104.7 75.5 %all-to-all-done.1 = bf16[16,16,64,128]{3,2,1,0:T(8,128)(2,1)} async-done(((bf16[16,16,64,128]{3,2,1,0:T(8,128)(2,1)}), bf16[16,16,64,128]{3,2,1,0:T(8,128)(2,1)}, u32[]{:S(2)}, u32[]{:S(2)}) %all-to-all-start.1) | async-done | bytes 4194336 | tf_op jit(solution)/shard_map/all_to_all | solution.py:88
  180.2 4.4 gather_fusion.2
  184.5 3.8 bitcast_reduce_fusion
  188.3 1.3 fusion.4
  189.6 0.1 add_reduce_fusion
  189.7 0.1 slice_reduce_fusion
  189.8 0.2 fusion.21
  190.1 0.1 copy.15
  190.2 0.1 maximum_multiply_fusion
  190.3 4.4 multiply_convert_fusion
  194.7 3.0 broadcast_in_dim.58
  197.7 15.7 %scatter_fusion = bf16[256,64,128]{2,1,0:T(8,128)(2,1)} fusion(bf16[256,64,128]{2,1,0:T(8,128)(2,1)} %broadcast_in_dim.58, s32[128]{0:T(128)S(1)} %fusion.17, bf16[128,64,128]{2,1,0:T(8,128)(2,1)S(1)} %bitcast.57), kind=kCustom, calls=%fused_computation.4 | custom fusion | bytes 6291968 | tf_op jit(solution)/shard_map/scatter | solution.py:99
  213.4 19.7 %all-to-all-start.2 = ((bf16[16,16,64,128]{3,2,1,0:T(8,128)(2,1)}), bf16[16,16,64,128]{3,2,1,0:T(8,128)(2,1)}, u32[]{:S(2)}, u32[]{:S(2)}) async-start(bf16[16,16,64,128]{3,2,1,0:T(8,128)(2,1)} %bitcast.53), calls=%async_computation.3 | async-start | bytes 8388608 | tf_op jit(solution)/shard_map/all_to_all | solution.py:100
  233.1 0.2 all-reduce.2.cloned.1.call-start
  233.3 77.4 %all-to-all-done.2 = bf16[16,16,64,128]{3,2,1,0:T(8,128)(2,1)} async-done(((bf16[16,16,64,128]{3,2,1,0:T(8,128)(2,1)}), bf16[16,16,64,128]{3,2,1,0:T(8,128)(2,1)}, u32[]{:S(2)}, u32[]{:S(2)}) %all-to-all-start.2) | async-done | bytes 4194336 | tf_op jit(solution)/shard_map/all_to_all | solution.py:100
  310.8 6.5 %bitcast_convert_fusion = f32[256,64,128]{2,1,0:T(8,128)} fusion(bf16[16,16,64,128]{3,2,1,0:T(8,128)(2,1)} %all-to-all-done.2), kind=kLoop, calls=%fused_computation.6 | loop fusion | flops 2097152 | bytes 12582912 | tf_op jit(solution)/shard_map/convert_element_type | solution.py:107
  317.2 0.2 broadcast_in_dim.34
  317.5 26.3 %scatter_fusion.1 = f32[64,64,128]{2,1,0:T(8,128)S(1)} fusion(f32[64,64,128]{2,1,0:T(8,128)S(1)} %broadcast_in_dim.34, s32[256]{0:T(256)S(1)} %bitcast.59, f32[256,64,128]{2,1,0:T(8,128)} %bitcast_convert_fusion), kind=kCustom, calls=%fused_computation.5 | custom fusion | flops 2097152 | bytes 25166848 | tf_op jit(solution)/shard_map/scatter-add | solution.py:107
  343.7 2.2 fusion.2
  345.9 0.6 broadcast_in_dim.33
  346.5 1.0 copy-done.3
  347.5 2.6 constant_dynamic-update-slice_fusion.3
  350.2 1.9 copy-done.4
  352.1 0.8 collective-permute-start
  352.9 18.3 %collective-permute-done = bf16[4096,128]{1,0:T(8,128)(2,1)S(1)} collective-permute-done((bf16[4096,128]{1,0:T(8,128)(2,1)S(1)}, bf16[4096,128]{1,0:T(8,128)(2,1)S(1)}, u32[]{:S(2)}, u32[]{:S(2)}) %collective-permute-start) | collective-permute-done | bytes 1048608 | tf_op jit(solution)/shard_map/ppermute | solution.py:19
  371.1 0.0 collective-permute-start.1
  371.1 14.2 %collective-permute-done.1 = bf16[4096,128]{1,0:T(8,128)(2,1)S(1)} collective-permute-done((bf16[4096,128]{1,0:T(8,128)(2,1)S(1)}, bf16[4096,128]{1,0:T(8,128)(2,1)S(1)}, u32[]{:S(2)}, u32[]{:S(2)}) %collective-permute-start.1) | collective-permute-done | bytes 1048608 | tf_op jit(solution)/shard_map/ppermute | solution.py:19
  385.4 0.0 collective-permute-start.2
  385.4 1.0 constant_dynamic-update-slice_fusion.2
  386.4 1.1 constant_dynamic-update-slice_fusion.1
  387.5 12.1 %collective-permute-done.2 = bf16[4096,128]{1,0:T(8,128)(2,1)S(1)} collective-permute-done((bf16[4096,128]{1,0:T(8,128)(2,1)S(1)}, bf16[4096,128]{1,0:T(8,128)(2,1)S(1)}, u32[]{:S(2)}, u32[]{:S(2)}) %collective-permute-start.2) | collective-permute-done | bytes 1048608 | tf_op jit(solution)/shard_map/ppermute | solution.py:19
  399.6 1.1 constant_dynamic-update-slice_fusion
  400.7 6.8 %convolution_bitcast_fusion = f32[256,128]{0,1:T(8,128)} fusion(bf16[16384,128]{1,0:T(8,128)(2,1)} %constant_dynamic-update-slice_fusion, bf16[16384,256]{1,0:T(8,128)(2,1)} %param.5), kind=kOutput, calls=%fused_computation.20 | convolution fusion | flops 1073741824 | bytes 12713984 | tf_op jit(solution)/shard_map/dot_general | solution.py:50
  407.5 0.0 all-reduce.2.cloned.1.call-update
  407.5 0.5 broadcast_multiply_fusion.1
  408.1 44.1 %all-reduce.2.cloned.1.call-done = f32[256,128]{0,1:T(8,128)} async-done(((f32[256,128]{0,1:T(8,128)}), f32[256,128]{0,1:T(8,128)}) %all-reduce.2.cloned.1.call-update) | async-done | bytes 131088 | tf_op jit(solution)/shard_map/psum | solution.py:112
  452.2 1.7 copy.16
  (18 shorter events, 0.1 us)
Async XLA Ops:
  7.2 0.8 copy-start
  7.2 84.4 %reduce-scatter.2.cloned.1.call-start = ((), (), s32[]{:S(2)}) async-start(), calls=%async_computation.4 | async-start | bytes 10485760 | tf_op jit(solution)/shard_map/reduce_scatter | solution.py:66
  16.9 0.7 copy-start.7
  91.5 2.4 copy-start.2
  97.7 82.5 %all-to-all-start.1 = ((bf16[16,16,64,128]{3,2,1,0:T(8,128)(2,1)}), bf16[16,16,64,128]{3,2,1,0:T(8,128)(2,1)}, u32[]{:S(2)}, u32[]{:S(2)}) async-start(bf16[16,16,64,128]{3,2,1,0:T(8,128)(2,1)} %bitcast.55), calls=%async_computation.2 | async-start | bytes 8388608 | tf_op jit(solution)/shard_map/all_to_all | solution.py:88
  102.5 0.7 copy-start.1
  180.2 4.4 copy-start.6
  194.7 3.0 copy-start.5
  213.4 97.4 %all-to-all-start.2 = ((bf16[16,16,64,128]{3,2,1,0:T(8,128)(2,1)}), bf16[16,16,64,128]{3,2,1,0:T(8,128)(2,1)}, u32[]{:S(2)}, u32[]{:S(2)}) async-start(bf16[16,16,64,128]{3,2,1,0:T(8,128)(2,1)} %bitcast.53), calls=%async_computation.3 | async-start | bytes 8388608 | tf_op jit(solution)/shard_map/all_to_all | solution.py:100
  233.1 219.1 %all-reduce.2.cloned.1.call-start = ((), (), s32[]{:S(2)}) async-start(), calls=%async_computation.5 | async-start | bytes 262144 | tf_op jit(solution)/shard_map/psum | solution.py:112
  345.9 1.6 copy-start.3
  350.2 1.9 copy-start.4
  352.1 19.0 %collective-permute-start = (bf16[4096,128]{1,0:T(8,128)(2,1)S(1)}, bf16[4096,128]{1,0:T(8,128)(2,1)S(1)}, u32[]{:S(2)}, u32[]{:S(2)}) collective-permute-start(bf16[4096,128]{1,0:T(8,128)(2,1)S(1)} %get-tuple-element.24), channel_id=1, source_target_pairs={{0,1},{1,2},{2,3},{3,0},{4,5},{5,6},{6,7},{7,4},{8,9},{9,10},{10,1... | collective-permute-start | bytes 3145736 | tf_op jit(solution)/shard_map/ppermute | solution.py:19
  371.1 14.2 %collective-permute-start.1 = (bf16[4096,128]{1,0:T(8,128)(2,1)S(1)}, bf16[4096,128]{1,0:T(8,128)(2,1)S(1)}, u32[]{:S(2)}, u32[]{:S(2)}) collective-permute-start(bf16[4096,128]{1,0:T(8,128)(2,1)S(1)} %collective-permute-done), channel_id=1, source_target_pairs={{0,1},{1,2},{2,3},{3,0},{4,5},{5,6},{6,7},{7,4},{8,9},{9,10},{10,1... | collective-permute-start | bytes 3145736 | tf_op jit(solution)/shard_map/ppermute | solution.py:19
  385.4 14.2 %collective-permute-start.2 = (bf16[4096,128]{1,0:T(8,128)(2,1)S(1)}, bf16[4096,128]{1,0:T(8,128)(2,1)S(1)}, u32[]{:S(2)}, u32[]{:S(2)}) collective-permute-start(bf16[4096,128]{1,0:T(8,128)(2,1)S(1)} %collective-permute-done.1), channel_id=1, source_target_pairs={{0,1},{1,2},{2,3},{3,0},{4,5},{5,6},{6,7},{7,4},{8,9},{9,10},{10,1... | collective-permute-start | bytes 3145736 | tf_op jit(solution)/shard_map/ppermute | solution.py:19
Sparse Core Ops, SparseCore 0:
  17.1 74.3 reduce-scatter.1
  407.7 44.4 all-reduce.1
